TPU v7x, 128 devices: a whole 4x4x4 slice. The times are simulated.
128 devices in a mesh: seq: 4 (over x), exp: 32 (over y, z, core).
Axes of the slice: x: 4, y: 4, z: 4, core: 2. Of those that a mesh axis runs over, the one named last changes fastest.
Arguments:
- resid: bfloat16 [32, 384, 2048], P('exp', 'seq'), may hold values from -6 to 6
- qkv: bfloat16 [32, 384, 6144], P('exp', 'seq'), may hold values from -8 to 8
- w_out: bfloat16 [2048, 2048], P('seq'), may hold values from -0.125 to 0.125
- norm_gain: float32 [2048], replicated, may hold values from 0.1 to 1.9
- router_w: bfloat16 [2048, 64], replicated, may hold values from -0.125 to 0.125
- expert_ids: int32 [32, 384, 6], P('exp'), may hold values from 0 to 63, all different within a row; in each aligned block of 96 rows (0 to 95, 96 to 191, ..., all dimensions but the last counted through in order) at most 12 rows name the same one
- w_gate_up: bfloat16 [64, 2048, 2, 1408], P('exp', None, None, 'seq'), may hold values from -0.125 to 0.125
- w_down: bfloat16 [64, 1408, 2048], P('exp', 'seq'), may hold values from -0.15625 to 0.15625
Outputs:
- layer_out: bfloat16 [32, 384, 2048], P('exp', 'seq')
Inputs may be any that keep to these rules, and one draw needn't show every extreme that they name: `expert_ids`: each point names 6 different experts. In each aligned block of 96 points (the points of one device, in the order of sets and then points), no expert is named by more than 12 points, and in every draw some expert is named by exactly 12 points of some block.
All inputs are finite; a program needn't handle non-finite values.
Results may differ from a plain program's by a relative error of at most 0.0065.
Values may be sent and summed in bfloat16 or wider, within the bound.
No kernel may reach another device: no remote copies, remote signals or barrier semaphores. Data moves between devices by JAX's collectives and lax.ppermute only.
A program may use at most 128 MiB of HBM per device.

v0:
```python
import math
import jax
import jax.numpy as jnp
from jax import lax
from jax.sharding import PartitionSpec as P

H = 16
HD = 128
EXPERTS = 64
epsilon = 1e-05


def gate_weights(normed_rows, router_w, chosen):
    logits = jnp.dot(normed_rows, router_w, preferred_element_type=jnp.float32)
    match = chosen[:, :, None] == jnp.arange(logits.shape[1], dtype=jnp.int32)[None, None, :]
    picked = jnp.sum(jnp.where(match, logits[:, None, :], jnp.zeros((), logits.dtype)), axis=-1)
    squashed = jax.nn.sigmoid(picked)
    return squashed / jnp.sum(squashed, axis=-1, keepdims=True)


def slot_ranks(chosen, block_rows, experts):
    blocks = chosen.shape[0] // block_rows
    width = block_rows * chosen.shape[1]
    grouped = chosen.reshape(blocks, width)
    hits = (grouped[:, :, None] == jnp.arange(experts, dtype=jnp.int32)[None, None, :]).astype(
        jnp.bfloat16
    )
    lower = jnp.arange(width)[:, None] >= jnp.arange(width)[None, :]
    counts = jnp.einsum(
        "ij,bje->bie", lower.astype(jnp.bfloat16), hits, preferred_element_type=jnp.float32
    )
    ranks = jnp.sum(counts * hits.astype(jnp.float32), axis=-1) - 1
    return ranks.astype(jnp.int32).reshape(chosen.shape)


def expert_part(received, w_gate_up, w_down):
    both = jnp.einsum("aend,edgf->aengf", received, w_gate_up, preferred_element_type=jnp.float32)
    hidden = (jax.nn.silu(both[:, :, :, 0]) * both[:, :, :, 1]).astype(jnp.bfloat16)
    return jnp.einsum("aenf,efd->aend", hidden, w_down, preferred_element_type=jnp.float32)


def scatter_rows(normed_rows, slot_index, buffer_rows):
    slots = jnp.arange(buffer_rows, dtype=jnp.int32)
    select = jnp.sum((slot_index[None, :, :] == slots[:, None, None]).astype(jnp.bfloat16), axis=-1)
    return jnp.dot(select, normed_rows, preferred_element_type=jnp.float32).astype(jnp.bfloat16)


def combine_rows(out_table, slot_index, gate_vals):
    slots = jnp.arange(out_table.shape[0], dtype=jnp.int32)
    weights = jnp.sum(
        jnp.where(slot_index[:, :, None] == slots[None, None, :], gate_vals[:, :, None], 0.0),
        axis=1,
    )
    high = weights.astype(jnp.bfloat16)
    low = (weights - high.astype(jnp.float32)).astype(jnp.bfloat16)
    return jnp.dot(high, out_table, preferred_element_type=jnp.float32) + jnp.dot(
        low, out_table, preferred_element_type=jnp.float32
    )


def on_device(resid, qkv, w_out, norm_gain, router_w, expert_ids, w_gate_up, w_down):
    row_count = resid.shape[1]
    model_width = resid.shape[2]
    seq_size = lax.axis_size("seq")
    exp_size = lax.axis_size("exp")
    seq_length = row_count * seq_size
    head_local = H // seq_size
    local_width = head_local * HD
    packed = qkv.reshape(row_count, 3, seq_size, local_width)
    regrouped = lax.all_to_all(packed, "seq", split_axis=2, concat_axis=0, tiled=True)
    queries = regrouped[:, 0, 0].reshape(seq_length, head_local, HD)
    keys_all = regrouped[:, 1, 0].reshape(seq_length, head_local, HD)
    values_all = regrouped[:, 2, 0].reshape(seq_length, head_local, HD)
    query_block = min(seq_length, 512)

    def attend_block(query_rows):
        scores = jnp.einsum(
            "qhd,khd->hqk", query_rows, keys_all, preferred_element_type=jnp.float32
        ) / math.sqrt(HD)
        weights = jax.nn.softmax(scores, axis=-1).astype(jnp.bfloat16)
        mixed_heads = jnp.einsum(
            "hqk,khd->qhd", weights, values_all, preferred_element_type=jnp.float32
        )
        return mixed_heads.reshape(query_rows.shape[0], local_width).astype(jnp.bfloat16)

    attended = lax.map(
        attend_block, queries.reshape(seq_length // query_block, query_block, head_local, HD)
    )
    attended = attended.reshape(seq_length, local_width)
    back = lax.all_to_all(
        attended.reshape(seq_length, 1, local_width), "seq", split_axis=0, concat_axis=1, tiled=True
    )
    point_rows = back.reshape(row_count, model_width)
    projected = jnp.dot(
        point_rows,
        lax.all_gather(w_out, "seq", axis=0, tiled=True),
        preferred_element_type=jnp.float32,
    )
    mixed = resid[0].astype(jnp.float32) + projected
    meansq = jnp.mean(mixed * mixed, axis=-1, keepdims=True)
    normed = (mixed * lax.rsqrt(meansq + epsilon) * norm_gain).astype(jnp.bfloat16)
    exp_local = w_gate_up.shape[0]
    slot_cap = row_count // 8
    gathered = lax.all_gather(normed, "seq", axis=0, tiled=True)
    chosen = expert_ids[0]
    gate_vals = gate_weights(gathered, router_w, chosen)
    ranks = slot_ranks(chosen, row_count, EXPERTS)
    owner_rows = seq_size * slot_cap
    source_block = (jnp.arange(seq_length, dtype=jnp.int32) // row_count)[:, None]
    slot_index = chosen * owner_rows + source_block * slot_cap + ranks
    outgoing = scatter_rows(gathered, slot_index, EXPERTS * owner_rows)
    outgoing = outgoing.reshape(exp_size, exp_local, owner_rows, model_width)
    partial_out = expert_part(
        lax.all_to_all(outgoing, "exp", split_axis=0, concat_axis=0, tiled=True), w_gate_up, w_down
    ).astype(jnp.bfloat16)
    returned = lax.all_to_all(partial_out, "exp", split_axis=0, concat_axis=0, tiled=True)
    out_table = returned.reshape(-1, model_width)
    expert_sum = lax.psum_scatter(
        combine_rows(out_table, slot_index, gate_vals).astype(jnp.bfloat16),
        "seq",
        scatter_dimension=0,
        tiled=True,
    ).astype(jnp.float32)
    return (mixed + expert_sum).astype(jnp.bfloat16).reshape(1, row_count, model_width)


def solution(mesh):
    in_specs = (
        P("exp", "seq", None),
        P("exp", "seq", None),
        P("seq", None),
        P(),
        P(),
        P("exp", None, None),
        P("exp", None, None, "seq"),
        P("exp", "seq", None),
    )
    out_specs = P("exp", "seq", None)
    return jax.shard_map(
        on_device, mesh=mesh, in_specs=in_specs, out_specs=out_specs, check_vma=False
    )
```

profile of v0, /device:TPU:0, one launch (start us, length us, event | category | flops | bytes accessed | tf_op | source)
XLA Modules:
  0.0 582.8 jit_solution(9345225432618470734)
XLA Ops:
  7.3 2.9 reshape.139
  10.2 1.5 copy.111
  11.7 27.4 %all_to_all.43 = bf16[96,3,4,512]{3,0,1,2:T(8,128)(2,1)S(1)} all-to-all(bf16[96,3,4,512]{3,0,1,2:T(8,128)(2,1)S(1)} %copy.111), channel_id=1, replica_groups=mesh['seq'=4,'exp'=32] {'seq'}, dimensions={2} | all-to-all | bytes 2359296 | tf_op jit(solution)/shard_map/all_to_all | solution.py:70
  39.2 1.0 fusion.48
  40.2 1.9 copy.117
  42.2 1.9 copy.113
  44.1 0.9 copy.114
  45.0 3.5 fusion.49
  48.5 2.2 convolution_convert_fusion.1
  51.2 1.5 reduce.1
  52.7 1.2 copy.150
  53.9 1.0 reshape.149
  54.9 15.5 %all_to_all.44 = bf16[4,2,24576]{2,1,0:T(2,128)(2,1)S(1)} all-to-all(bf16[4,2,24576]{2,1,0:T(2,128)(2,1)} %reshape.149), channel_id=1, replica_groups=mesh['seq'=4,'exp'=32] {'seq'}, dimensions={0} | all-to-all | bytes 786432 | tf_op jit(solution)/shard_map/all_to_all | solution.py:90
  70.4 1.7 reshape.150
  72.1 1.2 copy.138
  73.7 30.5 %all-gather.3.cloned.1.call-done = bf16[2048,2048]{1,0:T(8,128)(2,1)} async-done(((bf16[512,2048]{1,0:T(8,128)(2,1)}), bf16[2048,2048]{1,0:T(8,128)(2,1)}) %all-gather.3.cloned.1.call-update) | async-done | bytes 8388624 | tf_op jit(solution)/shard_map/all_gather | solution.py:96
  104.1 5.0 multiply_reduce_fusion.1
  109.2 0.9 copy-done.2
  112.2 5.6 fusion.2
  117.8 20.6 %all-gather.5.cloned.1.call-done = bf16[384,2048]{1,0:T(8,128)(2,1)} async-done(((bf16[96,2048]{1,0:T(8,128)(2,1)}), bf16[384,2048]{1,0:T(8,128)(2,1)}) %all-gather.5.cloned.1.call-update) | async-done | bytes 1572880 | tf_op jit(solution)/shard_map/all_gather | solution.py:104
  138.4 8.7 %convolution_convert_fusion = bf16[3072,2048]{1,0:T(8,128)(2,1)S(1)} fusion(bf16[3072,384]{1,0:T(8,128)(2,1)} %fusion.2, bf16[384,2048]{1,0:T(8,128)(2,1)} %all-gather.5.cloned.1.call-done), kind=kOutput, calls=%fused_computation.9 | convolution fusion | flops 4838129664 | bytes 16515072 | tf_op jit(solution)/shard_map/dot_general | solution.py:45
  147.1 147.5 %all_to_all.45 = bf16[32,2,48,2048]{3,2,1,0:T(8,128)(2,1)} all-to-all(bf16[32,2,48,2048]{3,2,1,0:T(8,128)(2,1)S(1)} %bitcast.99), channel_id=1, replica_groups=mesh['seq'=4,'exp'=32] {'exp'}, dimensions={0} | all-to-all | bytes 25165824 | tf_op jit(solution)/shard_map/all_to_all | solution.py:114
  294.6 16.0 %fusion.8 = f32[32,2,48,2,352]{4,2,3,0,1:T(8,128)} fusion(bf16[2,2048,2,352]{1,3,2,0:T(8,128)(2,1)} %param.14, bf16[32,2,48,2048]{3,2,1,0:T(8,128)(2,1)} %all_to_all.45), kind=kOutput, calls=%fused_computation.16 | convolution fusion | flops 8858370048 | bytes 27000832 | tf_op jit(solution)/shard_map/aend,edgf->aengf/dot_general | solution.py:37
  310.6 10.7 %convert_bitcast_fusion = bf16[32,2,48,2048]{3,2,0,1:T(8,128)(2,1)S(1)} fusion(bf16[2,352,2048]{2,1,0:T(8,128)(2,1)S(1)} %copy-done, f32[32,2,48,2,352]{4,2,3,0,1:T(8,128)} %fusion.8), kind=kOutput, calls=%fused_computation.8 | convolution fusion | flops 4441964544 | bytes 24117248 | tf_op jit(solution)/shard_map/aenf,efd->aend/dot_general | solution.py:39
  321.3 5.2 copy.128
  326.5 5.2 all-to-all-start.3
  333.2 8.6 %select_reduce_fusion = f32[384,3072]{1,0:T(8,128)} fusion(f32[384,6]{0,1:T(8,128)S(1)} %multiply_divide_fusion, s32[384,6]{0,1:T(8,128)S(1)} %copy.123), kind=kLoop, calls=%fused_computation.2 | loop fusion | flops 20054016 | bytes 4737024 | tf_op jit(solution)/shard_map/reduce_sum | solution.py:50
  341.7 167.1 %all-to-all-done.3 = bf16[32,2,48,2048]{3,2,1,0:T(8,128)(2,1)} async-done(((bf16[32,2,48,2048]{3,2,1,0:T(8,128)(2,1)}), bf16[32,2,48,2048]{3,2,1,0:T(8,128)(2,1)}, u32[]{:S(2)}, u32[]{:S(2)}) %all-to-all-start.3) | async-done | bytes 12582944 | tf_op jit(solution)/shard_map/all_to_all | solution.py:116
  508.9 11.0 %fusion.32 = f32[384,2048]{1,0:T(8,128)S(1)} fusion(bf16[3072,2048]{1,0:T(8,128)(2,1)} %bitcast.26, f32[384,3072]{1,0:T(8,128)} %select_reduce_fusion), kind=kOutput, calls=%fused_computation.33 | convolution fusion | flops 4833017856 | bytes 20447232 | tf_op jit(solution)/shard_map/dot_general | solution.py:56
  519.9 9.8 %add_convert_fusion = bf16[384,2048]{1,0:T(8,128)(2,1)} fusion(f32[384,2048]{1,0:T(8,128)S(1)} %fusion.32, bf16[3072,2048]{1,0:T(8,128)(2,1)} %bitcast.26, f32[384,3072]{1,0:T(8,128)S(1)} %copy-done.3), kind=kOutput, calls=%fused_computation.17 | convolution fusion | flops 4838129664 | bytes 22020096 | tf_op jit(solution)/shard_map/dot_general | solution.py:56
  529.7 44.4 %reduce-scatter.2.cloned.1.call-done = bf16[96,2048]{1,0:T(8,128)(2,1)} async-done(((bf16[384,2048]{1,0:T(8,128)(2,1)}), bf16[96,2048]{1,0:T(8,128)(2,1)}) %reduce-scatter.2.cloned.1.call-update) | async-done | bytes 393232 | tf_op jit(solution)/shard_map/reduce_scatter | solution.py:118
  574.2 2.1 fusion.36
  (44 shorter events, 5.2 us)
Async XLA Ops:
  6.5 304.1 %copy-start = (bf16[2,352,2048]{2,1,0:T(8,128)(2,1)S(1)}, bf16[2,352,2048]{2,1,0:T(8,128)(2,1)}, u32[]{:S(2)}) copy-start(bf16[2,352,2048]{2,1,0:T(8,128)(2,1)} %param.15) | copy-start | bytes 8650756
  6.5 97.6 %all-gather.3.cloned.1.call-start = ((), (), s32[]{:S(2)}) async-start(), calls=%async_computation.5 | async-start | bytes 10485760 | tf_op jit(solution)/shard_map/all_gather | solution.py:96
  7.3 131.1 %all-gather.5.cloned.1.call-start = ((), (), s32[]{:S(2)}) async-start(), calls=%async_computation.6 | async-start | bytes 1966080 | tf_op jit(solution)/shard_map/all_gather | solution.py:104
  104.1 6.0 %copy-start.7 = (f32[2048]{0:T(1024)S(1)}, f32[2048]{0:T(1024)}, u32[]{:S(2)}) copy-start(f32[2048]{0:T(1024)} %param.11) | copy-start | bytes 24580
  104.1 6.9 %copy-start.6 = (s32[1,384,6]{1,0,2:T(1,128)S(1)}, s32[1,384,6]{1,0,2:T(1,128)}, u32[]{:S(2)}) copy-start(s32[1,384,6]{1,0,2:T(1,128)} %param.13) | copy-start | bytes 27652
  109.1 1.0 copy-start.2
  326.5 5.9 %copy-start.4 = (bf16[384,2048]{1,0:T(8,128)(2,1)S(1)}, bf16[384,2048]{1,0:T(8,128)(2,1)}, u32[]{:S(2)}) copy-start(bf16[384,2048]{1,0:T(8,128)(2,1)} %all-gather.5.cloned.1.call-done) | copy-start | bytes 4718596
  326.5 5.9 %copy-start.5 = (bf16[2048,64]{0,1:T(8,128)(2,1)S(1)}, bf16[2048,64]{0,1:T(8,128)(2,1)}, u32[]{:S(2)}) copy-start(bf16[2048,64]{0,1:T(8,128)(2,1)} %param.12) | copy-start | bytes 786436
  326.5 182.3 %all-to-all-start.3 = ((bf16[32,2,48,2048]{3,2,1,0:T(8,128)(2,1)}), bf16[32,2,48,2048]{3,2,1,0:T(8,128)(2,1)}, u32[]{:S(2)}, u32[]{:S(2)}) async-start(bf16[32,2,48,2048]{3,2,1,0:T(8,128)(2,1)} %copy.128), calls=%async_computation.3 | async-start | bytes 25165824 | tf_op jit(solution)/shard_map/all_to_all | solution.py:116
  331.7 242.5 %reduce-scatter.2.cloned.1.call-start = ((), (), s32[]{:S(2)}) async-start(), calls=%async_computation.7 | async-start | bytes 1966080 | tf_op jit(solution)/shard_map/reduce_scatter | solution.py:118
  508.9 11.0 %copy-start.3 = (f32[384,3072]{1,0:T(8,128)S(1)}, f32[384,3072]{1,0:T(8,128)}, u32[]{:S(2)}) copy-start(f32[384,3072]{1,0:T(8,128)} %select_reduce_fusion) | copy-start | bytes 14155780
  519.9 56.3 %copy-start.1 = (bf16[2,352,2048]{2,1,0:T(8,128)(2,1)S(1)}, bf16[2,352,2048]{2,1,0:T(8,128)(2,1)}, u32[]{:S(2)}) copy-start(bf16[2,352,2048]{2,1,0:T(8,128)(2,1)} %param.15) | copy-start | bytes 8650756
Sparse Core Ops, SparseCore 0:
  9.0 95.0 all-gather.2
  111.1 27.2 all-gather.4
  529.9 44.2 reduce-scatter.1
where the time goes:
time: 583 us
  waiting for transfers between devices  263 us (45%)
  blocking collectives  190 us (33%)
  matrix products  68 us (12%)
  local copies, waits for them, and re-layouts  23.2 us (4%)
  other arithmetic  18.9 us (3%)
  between operations  13.3 us (2%)
    all_to_all x1, waiting for transfers between devices, on_device(): lax.all_to_all(partial_out, 'exp', split_axis=0, concat_axis=0, tiled=True)  167 us
    all_to_all x1, blocking collectives, on_device(): lax.all_to_all(outgoing, 'exp', split_axis=0, concat_axis=0, tiled=True)  148 us
    reduce_scatter x1, waiting for transfers between devices, on_device(): lax.psum_scatter(combine_rows(out_table, slot_index, gate_vals).astype(jn...  44.4 us
    all_gather x1, waiting for transfers between devices, on_device(): lax.all_gather(w_out, 'seq', axis=0, tiled=True)  30.5 us
    all_to_all x1, blocking collectives, on_device(): lax.all_to_all(packed, 'seq', split_axis=2, concat_axis=0, tiled=True)  27.4 us
    all_gather x1, waiting for transfers between devices, on_device(): gathered = lax.all_gather(normed, 'seq', axis=0, tiled=True)  20.6 us
    dot_general x1, matrix products, expert_part(): jnp.einsum('aend,edgf->aengf', received, w_gate_up, preferred_element_typ...  16 us
    all_to_all x1, blocking collectives, on_device(): lax.all_to_all(attended.reshape(seq_length, 1, local_width), 'seq', split...  15.5 us
  transfers between devices with their start and end apart: 4, of which 4 were waited for; matrix products, arithmetic and copies ran while one was open for 7% of the time, Pallas kernels for 0%

commit v1 on v0

--- a/solution.py
+++ b/solution.py
@@ -87,8 +87,18 @@
         attend_block, queries.reshape(seq_length // query_block, query_block, head_local, HD)
     )
     attended = attended.reshape(seq_length, local_width)
-    back = lax.all_to_all(
-        attended.reshape(seq_length, 1, local_width), "seq", split_axis=0, concat_axis=1, tiled=True
+    back = jnp.concatenate(
+        lax.all_to_all(
+            jnp.stack(
+                jnp.split(
+                    attended.reshape(seq_length, 1, local_width), lax.axis_size("seq"), axis=0
+                )
+            ),
+            "seq",
+            0,
+            0,
+        ),
+        axis=1,
     )
     point_rows = back.reshape(row_count, model_width)
     projected = jnp.dot(

time: 583 us -> 583 us (level)
  waiting for transfers between devices: 263 us -> 271 us
    all_gather x1, waiting for transfers between devices: 30.5 us -> 38 us  [on_device(): lax.all_gather(w_out, 'seq', axis=0, tiled=True)]
  transfers between devices with their start and end apart: 4 -> 4, of which waited for: 4 -> 4; matrix products, arithmetic and copies ran while one was open for 7% -> 6% of each run, Pallas kernels for 0% -> 0%
where the time goes in v1:
time: 583 us
  waiting for transfers between devices  271 us (46%)
  blocking collectives  189 us (32%)
  matrix products  68 us (12%)
  local copies, waits for them, and re-layouts  18.1 us (3%)
  other arithmetic  17.4 us (3%)
  between operations  13.4 us (2%)
    all_to_all x1, waiting for transfers between devices, on_device(): lax.all_to_all(partial_out, 'exp', split_axis=0, concat_axis=0, tiled=True)  167 us
    all_to_all x1, blocking collectives, on_device(): lax.all_to_all(outgoing, 'exp', split_axis=0, concat_axis=0, tiled=True)  148 us
    reduce_scatter x1, waiting for transfers between devices, on_device(): lax.psum_scatter(combine_rows(out_table, slot_index, gate_vals).astype(jn...  44.4 us
    all_gather x1, waiting for transfers between devices, on_device(): lax.all_gather(w_out, 'seq', axis=0, tiled=True)  38 us
    all_to_all x1, blocking collectives, on_device(): lax.all_to_all(packed, 'seq', split_axis=2, concat_axis=0, tiled=True)  27.4 us
    all_gather x1, waiting for transfers between devices, on_device(): gathered = lax.all_gather(normed, 'seq', axis=0, tiled=True)  20.6 us
    dot_general x1, matrix products, expert_part(): jnp.einsum('aend,edgf->aengf', received, w_gate_up, preferred_element_typ...  16 us
    all_to_all x1, blocking collectives, on_device(): lax.all_to_all(jnp.stack(jnp.split(attended.reshape(seq_length, 1, local_...  14.5 us
  transfers between devices with their start and end apart: 4, of which 4 were waited for; matrix products, arithmetic and copies ran while one was open for 6% of the time, Pallas kernels for 0%

profile of v1, /device:TPU:0, one launch (start us, length us, event | category | flops | bytes accessed | tf_op | source)
XLA Modules:
  0.0 582.8 jit_solution(17991028955438366877)
XLA Ops:
  6.5 0.7 all-gather.3.cloned.1.call-update
  7.3 2.9 reshape.144
  10.2 1.5 copy.130
  11.7 27.4 %all_to_all.33 = bf16[96,3,4,512]{3,0,1,2:T(8,128)(2,1)S(1)} all-to-all(bf16[96,3,4,512]{3,0,1,2:T(8,128)(2,1)S(1)} %copy.130), channel_id=1, replica_groups=mesh['seq'=4,'exp'=32] {'seq'}, dimensions={2} | all-to-all | bytes 2359296 | tf_op jit(solution)/shard_map/all_to_all | solution.py:70
  39.2 1.0 fusion.49
  40.2 1.9 copy.132
  42.2 1.9 copy.133
  44.1 0.9 copy.136
  45.0 3.5 fusion.51
  48.5 2.3 fusion.28
  51.3 14.5 %all_to_all.34 = bf16[4,96,1,512]{3,1,2,0:T(8,128)(2,1)S(1)} all-to-all(bf16[4,96,1,512]{3,1,2,0:T(8,128)(2,1)S(1)} %pad_maximum_fusion), channel_id=1, replica_groups=mesh['seq'=4,'exp'=32] {'seq'}, dimensions={0} | all-to-all | bytes 786432 | tf_op jit(solution)/shard_map/all_to_all | solution.py:91
  65.7 0.3 copy.143
  66.1 38.0 %all-gather.3.cloned.1.call-done = bf16[2048,2048]{1,0:T(8,128)(2,1)} async-done(((bf16[512,2048]{1,0:T(8,128)(2,1)}), bf16[2048,2048]{1,0:T(8,128)(2,1)}) %all-gather.3.cloned.1.call-update) | async-done | bytes 8388624 | tf_op jit(solution)/shard_map/all_gather | solution.py:106
  104.1 5.0 multiply_reduce_fusion.1
  109.2 0.9 copy-done.2
  110.1 0.9 multiply_convert_fusion
  111.3 0.5 fusion.29
  112.2 5.6 fusion.2
  117.8 20.6 %all-gather.5.cloned.1.call-done = bf16[384,2048]{1,0:T(8,128)(2,1)} async-done(((bf16[96,2048]{1,0:T(8,128)(2,1)}), bf16[384,2048]{1,0:T(8,128)(2,1)}) %all-gather.5.cloned.1.call-update) | async-done | bytes 1572880 | tf_op jit(solution)/shard_map/all_gather | solution.py:114
  138.4 8.7 %convolution_convert_fusion = bf16[3072,2048]{1,0:T(8,128)(2,1)S(1)} fusion(bf16[3072,384]{1,0:T(8,128)(2,1)} %fusion.2, bf16[384,2048]{1,0:T(8,128)(2,1)} %all-gather.5.cloned.1.call-done), kind=kOutput, calls=%fused_computation.9 | convolution fusion | flops 4838129664 | bytes 16515072 | tf_op jit(solution)/shard_map/dot_general | solution.py:45
  147.1 147.5 %all_to_all.35 = bf16[32,2,48,2048]{3,2,1,0:T(8,128)(2,1)} all-to-all(bf16[32,2,48,2048]{3,2,1,0:T(8,128)(2,1)S(1)} %bitcast.96), channel_id=1, replica_groups=mesh['seq'=4,'exp'=32] {'exp'}, dimensions={0} | all-to-all | bytes 25165824 | tf_op jit(solution)/shard_map/all_to_all | solution.py:124
  294.6 16.0 %fusion.8 = f32[32,2,48,2,352]{4,2,3,0,1:T(8,128)} fusion(bf16[2,2048,2,352]{1,3,2,0:T(8,128)(2,1)} %param.14, bf16[32,2,48,2048]{3,2,1,0:T(8,128)(2,1)} %all_to_all.35), kind=kOutput, calls=%fused_computation.16 | convolution fusion | flops 8858370048 | bytes 27000832 | tf_op jit(solution)/shard_map/aend,edgf->aengf/dot_general | solution.py:37
  310.6 10.7 %convert_bitcast_fusion = bf16[32,2,48,2048]{3,2,0,1:T(8,128)(2,1)S(1)} fusion(bf16[2,352,2048]{2,1,0:T(8,128)(2,1)S(1)} %copy-done, f32[32,2,48,2,352]{4,2,3,0,1:T(8,128)} %fusion.8), kind=kOutput, calls=%fused_computation.8 | convolution fusion | flops 4441964544 | bytes 24117248 | tf_op jit(solution)/shard_map/aenf,efd->aend/dot_general | solution.py:39
  321.3 5.2 copy.151
  326.5 5.2 all-to-all-start.3
  332.4 0.6 fusion.52
  333.2 8.6 %select_reduce_fusion = f32[384,3072]{1,0:T(8,128)} fusion(f32[384,6]{0,1:T(8,128)S(1)} %multiply_divide_fusion, s32[384,6]{0,1:T(8,128)S(1)} %copy.146), kind=kLoop, calls=%fused_computation.2 | loop fusion | flops 20054016 | bytes 4737024 | tf_op jit(solution)/shard_map/reduce_sum | solution.py:50
  341.7 167.1 %all-to-all-done.3 = bf16[32,2,48,2048]{3,2,1,0:T(8,128)(2,1)} async-done(((bf16[32,2,48,2048]{3,2,1,0:T(8,128)(2,1)}), bf16[32,2,48,2048]{3,2,1,0:T(8,128)(2,1)}, u32[]{:S(2)}, u32[]{:S(2)}) %all-to-all-start.3) | async-done | bytes 12582944 | tf_op jit(solution)/shard_map/all_to_all | solution.py:126
  508.9 11.0 %fusion.33 = f32[384,2048]{1,0:T(8,128)S(1)} fusion(bf16[3072,2048]{1,0:T(8,128)(2,1)} %bitcast.25, f32[384,3072]{1,0:T(8,128)} %select_reduce_fusion), kind=kOutput, calls=%fused_computation.34 | convolution fusion | flops 4833017856 | bytes 20447232 | tf_op jit(solution)/shard_map/dot_general | solution.py:56
  519.9 9.8 %add_convert_fusion = bf16[384,2048]{1,0:T(8,128)(2,1)} fusion(f32[384,2048]{1,0:T(8,128)S(1)} %fusion.33, bf16[3072,2048]{1,0:T(8,128)(2,1)} %bitcast.25, f32[384,3072]{1,0:T(8,128)S(1)} %copy-done.3), kind=kOutput, calls=%fused_computation.17 | convolution fusion | flops 4838129664 | bytes 22020096 | tf_op jit(solution)/shard_map/dot_general | solution.py:56
  529.7 44.4 %reduce-scatter.2.cloned.1.call-done = bf16[96,2048]{1,0:T(8,128)(2,1)} async-done(((bf16[384,2048]{1,0:T(8,128)(2,1)}), bf16[96,2048]{1,0:T(8,128)(2,1)}) %reduce-scatter.2.cloned.1.call-update) | async-done | bytes 393232 | tf_op jit(solution)/shard_map/reduce_scatter | solution.py:128
  574.2 2.1 fusion.37
  (48 shorter events, 2.2 us)
Async XLA Ops:
  6.5 304.1 %copy-start = (bf16[2,352,2048]{2,1,0:T(8,128)(2,1)S(1)}, bf16[2,352,2048]{2,1,0:T(8,128)(2,1)}, u32[]{:S(2)}) copy-start(bf16[2,352,2048]{2,1,0:T(8,128)(2,1)} %param.15) | copy-start | bytes 8650756
  6.5 97.6 %all-gather.3.cloned.1.call-start = ((), (), s32[]{:S(2)}) async-start(), calls=%async_computation.5 | async-start | bytes 10485760 | tf_op jit(solution)/shard_map/all_gather | solution.py:106
  7.3 131.1 %all-gather.5.cloned.1.call-start = ((), (), s32[]{:S(2)}) async-start(), calls=%async_computation.6 | async-start | bytes 1966080 | tf_op jit(solution)/shard_map/all_gather | solution.py:114
  104.1 6.0 %copy-start.7 = (f32[2048]{0:T(1024)S(1)}, f32[2048]{0:T(1024)}, u32[]{:S(2)}) copy-start(f32[2048]{0:T(1024)} %param.11) | copy-start | bytes 24580
  104.1 6.9 %copy-start.6 = (s32[1,384,6]{1,0,2:T(1,128)S(1)}, s32[1,384,6]{1,0,2:T(1,128)}, u32[]{:S(2)}) copy-start(s32[1,384,6]{1,0,2:T(1,128)} %param.13) | copy-start | bytes 27652
  109.1 1.0 copy-start.2
  326.5 5.9 %copy-start.4 = (bf16[384,2048]{1,0:T(8,128)(2,1)S(1)}, bf16[384,2048]{1,0:T(8,128)(2,1)}, u32[]{:S(2)}) copy-start(bf16[384,2048]{1,0:T(8,128)(2,1)} %all-gather.5.cloned.1.call-done) | copy-start | bytes 4718596
  326.5 5.9 %copy-start.5 = (bf16[2048,64]{0,1:T(8,128)(2,1)S(1)}, bf16[2048,64]{0,1:T(8,128)(2,1)}, u32[]{:S(2)}) copy-start(bf16[2048,64]{0,1:T(8,128)(2,1)} %param.12) | copy-start | bytes 786436
  326.5 182.3 %all-to-all-start.3 = ((bf16[32,2,48,2048]{3,2,1,0:T(8,128)(2,1)}), bf16[32,2,48,2048]{3,2,1,0:T(8,128)(2,1)}, u32[]{:S(2)}, u32[]{:S(2)}) async-start(bf16[32,2,48,2048]{3,2,1,0:T(8,128)(2,1)} %copy.151), calls=%async_computation.3 | async-start | bytes 25165824 | tf_op jit(solution)/shard_map/all_to_all | solution.py:126
  331.7 242.5 %reduce-scatter.2.cloned.1.call-start = ((), (), s32[]{:S(2)}) async-start(), calls=%async_computation.7 | async-start | bytes 1966080 | tf_op jit(solution)/shard_map/reduce_scatter | solution.py:128
  508.9 11.0 %copy-start.3 = (f32[384,3072]{1,0:T(8,128)S(1)}, f32[384,3072]{1,0:T(8,128)}, u32[]{:S(2)}) copy-start(f32[384,3072]{1,0:T(8,128)} %select_reduce_fusion) | copy-start | bytes 14155780
  519.9 56.3 %copy-start.1 = (bf16[2,352,2048]{2,1,0:T(8,128)(2,1)S(1)}, bf16[2,352,2048]{2,1,0:T(8,128)(2,1)}, u32[]{:S(2)}) copy-start(bf16[2,352,2048]{2,1,0:T(8,128)(2,1)} %param.15) | copy-start | bytes 8650756
Sparse Core Ops, SparseCore 0:
  9.0 95.0 all-gather.2
  111.1 27.2 all-gather.4
  529.9 44.2 reduce-scatter.1
